TPU v7x, 256 devices: a whole 4x4x8 slice. The times are simulated.
256 devices in a mesh: seq: 64 (over z, y, x_lo), head: 4 (over x_hi, core).
Axes of the slice: x: 4 (x_hi: 2, x_lo: 2; x = x_hi * 2 + x_lo), y: 4, z: 8, core: 2. Of those that a mesh axis runs over, the one named last changes fastest.
Arguments:
- features: bfloat16 [8192, 960], P('seq', 'head'), may hold values from -36 to 36
- conv_weight: bfloat16 [960, 120, 128], P('head'), may hold values from -0.046875 to 0.046875
- ln_gain: float32 [960], replicated, may hold values from 0.5 to 1.5
- ln_bias: float32 [960], replicated, may hold values from -4 to 4
- query_weight: bfloat16 [8, 115200], P('head'), may hold values from -0.875 to 0.875
- key_weight: bfloat16 [8, 115200], P('head'), may hold values from -0.875 to 0.875
- value_weight: bfloat16 [8, 115200], P('head'), may hold values from -0.1875 to 0.1875
- out_weight: bfloat16 [960, 960], P('head'), may hold values from -0.1875 to 0.1875
- proj_weight: bfloat16 [960, 1024], P(None, 'head'), may hold values from -0.10085894 to 0.10085894
- targets: bfloat16 [8192, 1024], P('seq', 'head'), may hold values from -3.125 to 3.125
- mask_positions: int32 [1024], P('seq'), may hold values from 0 to 8191, as said below
- distractors: int32 [1024, 100], P('seq'), may hold values from 0 to 8191, as said below
- loss_weight: float32 [1024], P('seq'), may hold values from 0.2 to 2
Outputs:
- encoded: bfloat16 [8192, 960], P('seq', 'head')
- proj_grad: float32 [960, 1024], P(None, 'head')
- target_grad: float32 [8192, 1024], P('seq', 'head')
Inputs may be any that keep to these rules, and one draw needn't show every extreme that they name: `mask_positions`: the entries of aligned block d of 16 are distinct frames of d * 128 to (d + 1) * 128 - 1. `distractors`: call value // 128 the block of an entry. In every aligned block of 16 rows exactly 50 entries name one block, the same block for all row blocks and drawn from the seed; the remaining 16 * 100 - 50 entries of the row block are spread over the other blocks as evenly as possible.
All inputs are finite; a program needn't handle non-finite values.
Results may differ from a plain program's by a relative error of at most 0.007.
Values may be sent and summed in bfloat16 or wider, within the bound.
No kernel may reach another device: no remote copies, remote signals or barrier semaphores. Data moves between devices by JAX's collectives and lax.ppermute only.
A program may use at most 128 MiB of HBM per device.

v0:
```python
import math
import jax
import jax.numpy as jnp
from jax import lax
from jax.sharding import PartitionSpec as P

TAPS = 128
NORM_EPS = 1e-05
EPSILON = 1e-06
SOFTMAX_WARMTH = 0.1


def with_halo(shard, sides, width):
    for axis, dim in sides:
        size, length = (lax.axis_size(axis), shard.shape[dim])
        up = [(i, (i + 1) % size) for i in range(size - 1)]
        down = [(j, i) for i, j in up]
        last = lax.slice_in_dim(shard, length - width, length, axis=dim)
        first = lax.slice_in_dim(shard, 0, width, axis=dim)
        before = lax.ppermute(last, axis, up)
        after = lax.ppermute(first, axis, down)
        shard = jnp.concatenate([before, shard, after], axis=dim)
    return shard


def layer_norm(hidden, gain_terms, bias_terms):
    wide = hidden.astype(jnp.float32)
    center = jnp.mean(wide, axis=-1, keepdims=True)
    spread = jnp.mean((wide - center) ** 2, axis=-1, keepdims=True)
    return ((wide - center) * lax.rsqrt(spread + NORM_EPS) * gain_terms + bias_terms).astype(
        jnp.bfloat16
    )


def head_project(normed, flat_weight, head_count, head_dim):
    full_width = normed.shape[1]
    head_weight = flat_weight.reshape(head_count, full_width, head_dim)
    result = jnp.einsum("tw,hwd->thd", normed, head_weight, preferred_element_type=jnp.float32)
    return result.astype(jnp.bfloat16)


def contrast_terms(products, target_sq, context_sq, weight_matrix):
    inv_context = lax.rsqrt(context_sq + EPSILON)
    inv_target = lax.rsqrt(target_sq + EPSILON)
    cosine_scores = products * inv_context[:, None] * inv_target
    exponentiated = jnp.exp(cosine_scores / SOFTMAX_WARMTH)
    softmax_shares = exponentiated / jnp.sum(exponentiated, axis=1, keepdims=True)
    leading_term = (lax.broadcasted_iota(jnp.int32, softmax_shares.shape, 1) == 0).astype(
        jnp.float32
    )
    logit_slope = weight_matrix[:, None] * (softmax_shares - leading_term) / SOFTMAX_WARMTH
    along = logit_slope * inv_context[:, None] * inv_target
    shrink = logit_slope * cosine_scores * inv_target * inv_target
    spread = jnp.sum(logit_slope * cosine_scores, axis=1) * inv_context * inv_context
    return (along, shrink, spread)


def attend_block(running, key_block, value_block, query_heads, head_count, score_scale):
    numer, denom, highest = running
    row_count = key_block.shape[0]
    key_heads = key_block.reshape(row_count, head_count, -1)
    value_heads = value_block.reshape(row_count, head_count, -1)
    scores = (
        jnp.einsum("qhd,khd->hqk", query_heads, key_heads, preferred_element_type=jnp.float32)
        * score_scale
    )
    new_high = jnp.maximum(highest, jnp.max(scores, axis=2))
    factor = jnp.exp(highest - new_high)
    weights = jnp.exp(scores - new_high[:, :, None])
    denom = denom * factor + jnp.sum(weights, axis=2)
    numer = numer * factor[:, :, None] + jnp.einsum(
        "hqk,khd->hqd",
        weights.astype(jnp.bfloat16),
        value_heads,
        preferred_element_type=jnp.float32,
    )
    return (numer, denom, new_high)


def take_rows(asked, targets):
    return targets[jnp.maximum(asked, 0)]


def place_rows(asked_flat, rows_flat, frame_count):
    segment_ids = jnp.where(asked_flat >= 0, asked_flat, frame_count)
    return jax.ops.segment_sum(rows_flat, segment_ids, num_segments=frame_count + 1)[:frame_count]


def per_device(
    features,
    conv_weight,
    ln_gain,
    ln_bias,
    query_weight,
    key_weight,
    value_weight,
    out_weight,
    proj_weight,
    targets,
    mask_positions,
    distractors,
    loss_weight,
):
    frame_count, local_width = features.shape
    head_dim = conv_weight.shape[1]
    head_count = local_width // head_dim
    extended = with_halo(features, (("seq", 0),), TAPS // 2)
    position = lax.conv_general_dilated(
        extended[None],
        conv_weight,
        (1,),
        "VALID",
        dimension_numbers=("NWC", "OIW", "NWC"),
        feature_group_count=head_count,
        preferred_element_type=jnp.float32,
    )[0, :frame_count]
    hidden = (features.astype(jnp.float32) + jax.nn.gelu(position, approximate=False)).astype(
        jnp.bfloat16
    )
    normed = layer_norm(lax.all_gather(hidden, "head", axis=1, tiled=True), ln_gain, ln_bias)
    query_heads = head_project(normed, query_weight, head_count, head_dim)
    key_here = head_project(normed, key_weight, head_count, head_dim).reshape(
        frame_count, local_width
    )
    value_here = head_project(normed, value_weight, head_count, head_dim).reshape(
        frame_count, local_width
    )
    score_scale = 1.0 / math.sqrt(head_dim)
    initial = (
        jnp.zeros((head_count, frame_count, head_dim), jnp.float32),
        jnp.zeros((head_count, frame_count), jnp.float32),
        jnp.full((head_count, frame_count), -1e30, jnp.float32),
    )
    running = initial
    key_piece = lax.all_gather(key_here, "seq", axis=0, tiled=True)
    value_piece = lax.all_gather(value_here, "seq", axis=0, tiled=True)
    row_count = key_piece.shape[0]

    def advance(partial_value, blocks):
        return (
            attend_block(partial_value, blocks[0], blocks[1], query_heads, head_count, score_scale),
            None,
        )

    running, _ = lax.scan(
        advance,
        running,
        (
            key_piece.reshape(row_count // 512, 512, -1),
            value_piece.reshape(row_count // 512, 512, -1),
        ),
    )
    numer, denom, _ = running
    attended = (
        (numer / denom[:, :, None])
        .astype(jnp.bfloat16)
        .transpose(1, 0, 2)
        .reshape(frame_count, local_width)
    )
    branch = lax.psum_scatter(
        jnp.dot(attended, out_weight, preferred_element_type=jnp.float32).astype(jnp.bfloat16),
        "head",
        scatter_dimension=1,
        tiled=True,
    ).astype(jnp.float32)
    encoded = (hidden.astype(jnp.float32) + branch).astype(jnp.bfloat16)
    seq_index = lax.axis_index("seq")
    seq_count = lax.axis_size("seq")
    local_mask = mask_positions - seq_index * frame_count
    masked_full = lax.all_gather(encoded[local_mask], "head", axis=1, tiled=True)
    context = jnp.dot(masked_full, proj_weight, preferred_element_type=jnp.float32)
    masked_count, distract_count = distractors.shape
    request_count = masked_count * distract_count
    capacity = 2 * request_count // seq_count
    target_width = targets.shape[1]
    flat_dist = distractors.reshape(-1)
    owners = flat_dist // frame_count
    row_ids = flat_dist % frame_count
    owner_hits = (owners[:, None] == jnp.arange(seq_count, dtype=jnp.int32)[None, :]).astype(
        jnp.int32
    )
    earlier = jnp.cumsum(owner_hits, axis=0) - owner_hits
    slot_ids = jnp.sum(earlier * owner_hits, axis=1)
    buckets = owners * capacity + slot_ids
    requests = (
        jnp.full((seq_count * capacity,), -1, jnp.int32)
        .at[buckets]
        .set(row_ids)
        .reshape(seq_count, capacity)
    )
    positive = targets[local_mask]
    asked = lax.all_to_all(requests, "seq", split_axis=0, concat_axis=0, tiled=True)
    found = take_rows(asked, targets)
    returned = lax.all_to_all(found, "seq", split_axis=0, concat_axis=0, tiled=True)
    fetched = returned.reshape(seq_count * capacity, target_width)[buckets].reshape(
        masked_count, distract_count, target_width
    )
    cands = jnp.concatenate([positive[:, None, :], fetched], axis=1).astype(jnp.float32)
    products_here = jnp.einsum("me,mke->mk", context, cands, precision=lax.Precision.HIGHEST)
    target_sq_here = jnp.sum(cands * cands, axis=2)
    context_sq_here = jnp.sum(context * context, axis=1)
    products, target_sq, context_sq = lax.psum(
        (products_here, target_sq_here, context_sq_here), "head"
    )
    along, shrink, spread = contrast_terms(products, target_sq, context_sq, loss_weight)
    cand_grads = along[:, :, None] * context[:, None, :] - shrink[:, :, None] * cands
    context_grad = (
        jnp.einsum("mk,mke->me", along, cands, precision=lax.Precision.HIGHEST)
        - spread[:, None] * context
    )
    target_grad = (
        jnp.zeros((frame_count, target_width), jnp.float32).at[local_mask].add(cand_grads[:, 0])
    )
    outgoing = (
        jnp.zeros((seq_count * capacity, target_width), jnp.float32)
        .at[buckets]
        .set(cand_grads[:, 1:].reshape(request_count, target_width))
    )
    incoming = (
        lax.all_to_all(
            outgoing.reshape(seq_count, capacity, target_width).astype(jnp.bfloat16),
            "seq",
            split_axis=0,
            concat_axis=0,
            tiled=True,
        )
        .astype(jnp.float32)
        .reshape(seq_count * capacity, target_width)
    )
    target_grad = target_grad + place_rows(asked.reshape(-1), incoming, frame_count)
    proj_term = jnp.einsum(
        "mw,me->we", masked_full.astype(jnp.float32), context_grad, precision=lax.Precision.HIGHEST
    )
    proj_grad = lax.psum(proj_term, "seq")
    return (encoded, proj_grad, target_grad)


def solution(mesh):
    return jax.shard_map(
        per_device,
        mesh=mesh,
        in_specs=(
            P("seq", "head"),
            P("head", None, None),
            P(),
            P(),
            P("head", None),
            P("head", None),
            P("head", None),
            P("head", None),
            P(None, "head"),
            P("seq", "head"),
            P("seq"),
            P("seq", None),
            P("seq"),
        ),
        out_specs=(P("seq", "head"), P(None, "head"), P("seq", "head")),
        check_vma=False,
    )
```

profile of v0, /device:TPU:8, one launch (start us, length us, event | category | flops | bytes accessed | tf_op | source)
XLA Modules:
  0.0 1307.5 jit_solution(7271690625776360250)
XLA Ops:
  8.2 3.4 collective-permute-start
  11.6 3.3 collective-permute-start.1
  15.0 10.7 copy.41
  27.6 17.3 %fusion.67 = f32[1,129,2,120]{3,0,2,1:T(1,128)S(1)} fusion(bf16[1,256,2,120]{3,0,2,1:T(2,128)(2,1)S(1)} %copy.40, bf16[2,120,120,128]{2,1,0,3:T(8,128)(2,1)} %copy.41), kind=kOutput, calls=%fused_computation.135 | convolution fusion | flops 951091200 | bytes 7619520 | tf_op jit(solution)/shard_map/conv_general_dilated | solution.py:108
  45.3 7.2 all_gather.12
  57.4 18.1 %reduce-window.6 = s32[64,13,128]{2,1,0:T(8,128)S(1)} reduce-window(s32[64,13,128]{2,1,0:T(8,128)S(1)} %reshape.259, s32[]{:T(128)} %constant.57.clone.1), window={size=1x1x128 pad=0_0x0_0x127_0}, to_apply=%region_7.8 | reduce-window | flops 13524992 | bytes 851972 | tf_op jit(solution)/shard_map/reduce-window
  76.7 8.8 scatter_custom_fusion
  86.3 12.8 all-to-all-start
  100.6 7.8 all-to-all-done
  110.0 9.9 gather_fusion.2
  119.9 1.5 reshape.279
  121.4 6.3 all-to-all-start.1
  128.5 194.0 %all-gather.7.cloned.1.call-done = bf16[8192,240]{0,1:T(8,128)(2,1)} async-done(((bf16[128,240]{0,1:T(8,128)(2,1)}), bf16[8192,240]{0,1:T(8,128)(2,1)}) %all-gather.7.cloned.1.call-update) | async-done | bytes 3932176 | tf_op jit(solution)/shard_map/all_gather | solution.py:136
  322.5 4.4 copy.77
  326.9 243.4 %all-gather.5.cloned.1.call-done = bf16[8192,240]{0,1:T(8,128)(2,1)} async-done(((bf16[128,240]{0,1:T(8,128)(2,1)}), bf16[8192,240]{0,1:T(8,128)(2,1)}) %all-gather.5.cloned.1.call-update) | async-done | bytes 3932176 | tf_op jit(solution)/shard_map/all_gather | solution.py:135
  570.3 4.4 copy.78
  574.8 29.4 %while.15 = (s32[]{:T(128)}, f32[2,128,120]{1,2,0:T(8,128)S(1)}, f32[2,128]{1,0:T(2,128)S(1)}, f32[2,128]{1,0:T(2,128)S(1)}, bf16[16,512,240]{1,2,0:T(8,128)(2,1...) while((s32[]{:T(128)}, f32[2,128,120]{1,2,0:T(8,128)S(1)}, ...), condition=%wide.region_5.6_spmd.clone, body=%wide.region_2.5_spmd.clone.sunk | while | flops 63794432 | bytes 3371117 | solution.py:145
  606.0 2.5 reshape.253
  608.5 5.6 gather_fusion.3
  614.7 20.9 %reduce-scatter.2.cloned.1.call-done = bf16[128,240]{0,1:T(8,128)(2,1)} async-done(((bf16[128,960]{0,1:T(8,128)(2,1)}), bf16[128,240]{0,1:T(8,128)(2,1)}) %reduce-scatter.2.cloned.1.call-update) | async-done | bytes 61456 | tf_op jit(solution)/shard_map/reduce_scatter | solution.py:160
  637.1 6.7 all-gather.1
  645.1 13.6 %all-reduce.1 = (f32[16,101]{1,0:T(8,128)S(1)}, f32[16]{0:T(128)S(1)}, f32[16,101]{1,0:T(8,128)S(1)}) all-reduce(f32[16,101]{1,0:T(8,128)S(1)} %fusion.7, f32[16]{0:T(128)S(1)} %get-tuple-element.115, f32[16,101]{1,0:T(8,128)S(1)} %bitcast.173), channel_id=1, replica_groups=mesh['seq'=64,'head'=4] {'head'}, use_global_device_ids=true, to_apply=%region_15.16 | all-reduce | flops 3248 | bytes 25984 | tf_op jit(solution)/shard_map/psum | solution.py:202
  662.4 12.8 scatter_custom_fusion.1
  675.2 2.1 convert_element_type.73
  677.3 1.5 convert_element_type.74
  678.8 11.5 all-to-all-start.2
  691.2 1.6 fusion.43
  693.8 40.9 %all-to-all-done.2 = bf16[64,50,256]{2,1,0:T(8,128)(2,1)S(1)} async-done(((bf16[64,50,256]{2,1,0:T(8,128)(2,1)}), bf16[64,50,256]{2,1,0:T(8,128)(2,1)S(1)}, u32[]{:S(2)}, u32[]{:S(2)}) %all-to-all-start.2) | async-done | bytes 1638432 | tf_op jit(solution)/shard_map/all_to_all | solution.py:220
  734.8 1.9 reshape.314
  736.7 20.7 %scatter_custom_fusion.2 = f32[129,256]{1,0:T(8,128)S(1)} fusion(s32[3200]{0:T(1024)S(1)} %fusion.48, f32[3200,256]{1,0:T(8,128)} %reshape.314, f32[]{:T(128)} %constant.68.clone.1), kind=kCustom, calls=%fused_computation.78 | custom fusion | flops 819200 | bytes 132608 | tf_op jit(solution)/shard_map/scatter-add | solution.py:86
  758.1 540.6 %all-reduce.4.cloned.1.call-done = f32[960,256]{1,0:T(8,128)} async-done(((f32[960,256]{1,0:T(8,128)}), f32[960,256]{1,0:T(8,128)}) %all-reduce.4.cloned.1.call-update) | async-done | bytes 983056 | tf_op jit(solution)/shard_map/psum | solution.py:234
  1298.8 2.2 copy.94
  (226 shorter events, 53.9 us)
Async XLA Ops:
  7.2 597.1 %copy-start = (bf16[240,960]{1,0:T(8,128)(2,1)S(1)}, bf16[240,960]{1,0:T(8,128)(2,1)}, u32[]{:S(2)}) copy-start(bf16[240,960]{1,0:T(8,128)(2,1)} %param.22) | copy-start | bytes 1382404
  7.2 315.4 %all-gather.7.cloned.1.call-start = ((), (), s32[]{:S(2)}) async-start(), calls=%async_computation.5 | async-start | bytes 3993600 | tf_op jit(solution)/shard_map/all_gather | solution.py:136
  8.2 19.0 %collective-permute-start = (bf16[64,240]{0,1:T(8,128)(2,1)S(1)}, bf16[64,240]{0,1:T(8,128)(2,1)S(1)}, u32[]{:S(2)}, u32[]{:S(2)}) collective-permute-start(bf16[64,240]{0,1:T(8,128)(2,1)S(1)} %get-tuple-element.106), channel_id=1, source_target_pairs={{0,4},{4,8},{8,12},{12,16},{16,20},{20,24},{24,28},{28,32},{32,36}... | collective-permute-start | bytes 92168 | tf_op jit(solution)/shard_map/ppermute | solution.py:20
  11.6 15.6 %collective-permute-start.1 = (bf16[64,240]{0,1:T(8,128)(2,1)S(1)}, bf16[64,240]{0,1:T(8,128)(2,1)S(1)}, u32[]{:S(2)}, u32[]{:S(2)}) collective-permute-start(bf16[64,240]{0,1:T(8,128)(2,1)S(1)} %get-tuple-element.107), channel_id=1, source_target_pairs={{4,0},{8,4},{12,8},{16,12},{20,16},{24,20},{28,24},{32,28},{36,32}... | collective-permute-start | bytes 92168 | tf_op jit(solution)/shard_map/ppermute | solution.py:21
  15.0 10.8 copy-start.5
  25.7 1.5 copy-start.3
  27.6 25.3 %copy-start.12 = (f32[960]{0:T(1024)S(1)}, f32[960]{0:T(1024)}, u32[]{:S(2)}) copy-start(f32[960]{0:T(1024)} %param.18) | copy-start | bytes 11524
  27.6 25.3 %copy-start.13 = (f32[960]{0:T(1024)S(1)}, f32[960]{0:T(1024)}, u32[]{:S(2)}) copy-start(f32[960]{0:T(1024)} %param.17) | copy-start | bytes 11524
  44.9 9.4 copy-start.6
  54.1 3.0 copy-start.10
  54.1 516.2 %all-gather.5.cloned.1.call-start = ((), (), s32[]{:S(2)}) async-start(), calls=%async_computation.4 | async-start | bytes 3993600 | tf_op jit(solution)/shard_map/all_gather | solution.py:135
  75.8 23.3 %copy-start.7 = (bf16[2,115200]{1,0:T(2,128)(2,1)S(1)}, bf16[2,115200]{1,0:T(2,128)(2,1)}, u32[]{:S(2)}) copy-start(bf16[2,115200]{1,0:T(2,128)(2,1)} %param.19) | copy-start | bytes 1382404
  76.4 33.5 %copy-start.1 = (bf16[128,256]{1,0:T(8,128)(2,1)S(1)}, bf16[128,256]{1,0:T(8,128)(2,1)}, u32[]{:S(2)}) copy-start(bf16[128,256]{1,0:T(8,128)(2,1)} %param.24) | copy-start | bytes 196612
  86.3 22.2 %all-to-all-start = ((s32[64,1,50]{2,1,0:T(1,128)}), s32[64,1,50]{2,1,0:T(1,128)S(1)}, u32[]{:S(2)}, u32[]{:S(2)}) async-start(s32[64,1,50]{2,1,0:T(1,128)} %bitcast.24), calls=%async_computation.1 | async-start | bytes 65536 | tf_op jit(solution)/shard_map/all_to_all | solution.py:192
  121.4 484.6 %all-to-all-start.1 = ((bf16[64,50,256]{2,1,0:T(8,128)(2,1)}), bf16[64,50,256]{2,1,0:T(8,128)(2,1)}, u32[]{:S(2)}, u32[]{:S(2)}) async-start(bf16[64,50,256]{2,1,0:T(8,128)(2,1)} %reshape.279), calls=%async_computation.2 | async-start | bytes 3670016 | tf_op jit(solution)/shard_map/all_to_all | solution.py:194
  127.7 507.9 %reduce-scatter.2.cloned.1.call-start = ((), (), s32[]{:S(2)}) async-start(), calls=%async_computation.6 | async-start | bytes 307200 | tf_op jit(solution)/shard_map/reduce_scatter | solution.py:160
  574.8 30.6 %copy-start.14 = (s32[16]{0:T(128)S(1)}, s32[16]{0:T(128)}, u32[]{:S(2)}) copy-start(s32[16]{0:T(128)} %param.25) | copy-start | bytes 196
  614.1 29.9 %copy-start.4 = (bf16[960,256]{1,0:T(8,128)(2,1)S(1)}, bf16[960,256]{1,0:T(8,128)(2,1)}, u32[]{:S(2)}) copy-start(bf16[960,256]{1,0:T(8,128)(2,1)} %param.23) | copy-start | bytes 1474564
  614.3 44.5 %copy-start.11 = (f32[16]{0:T(128)S(1)}, f32[16]{0:T(128)}, u32[]{:S(2)}) copy-start(f32[16]{0:T(128)} %param.27) | copy-start | bytes 196
  636.4 23.3 %copy-start.8 = (bf16[128,240]{0,1:T(8,128)(2,1)}, bf16[128,240]{0,1:T(8,128)(2,1)S(1)}, u32[]{:S(2)}) copy-start(bf16[128,240]{0,1:T(8,128)(2,1)S(1)} %add_convert_fusion) | copy-start | bytes 184324
  659.7 1.2 copy-start.2
  678.8 56.0 %all-to-all-start.2 = ((bf16[64,50,256]{2,1,0:T(8,128)(2,1)}), bf16[64,50,256]{2,1,0:T(8,128)(2,1)S(1)}, u32[]{:S(2)}, u32[]{:S(2)}) async-start(bf16[64,50,256]{2,1,0:T(8,128)(2,1)} %convert_element_type.74), calls=%async_computation.3 | async-start | bytes 3670016 | tf_op jit(solution)/shard_map/all_to_all | solution.py:220
  690.2 608.5 %all-reduce.4.cloned.1.call-start = ((), (), s32[]{:S(2)}) async-start(), calls=%async_computation.7 | async-start | bytes 1966080 | tf_op jit(solution)/shard_map/psum | solution.py:234
  758.1 542.8 %copy-start.9 = (f32[128,256]{1,0:T(8,128)}, f32[128,256]{1,0:T(8,128)S(1)}, u32[]{:S(2)}) copy-start(f32[128,256]{1,0:T(8,128)S(1)} %scatter_custom_fusion.3) | copy-start | bytes 393220
Sparse Core Ops, SparseCore 0:
  54.2 268.2 all-gather.6
  324.8 245.4 all-gather.4
  605.4 30.1 reduce-scatter.1
  694.2 604.5 all-reduce.3
where the time goes:
time: 1310 us
  waiting for transfers between devices  1050 us (80%)
  local copies, waits for them, and re-layouts  97.4 us (7%)
  other arithmetic  49.3 us (4%)
  starting transfers between devices  38.1 us (3%)
  matrix products  32.3 us (2%)
  blocking collectives  27.5 us (2%)
  between operations  14.4 us (1%)
    psum x1, waiting for transfers between devices, per_device(): proj_grad = lax.psum(proj_term, 'seq')  541 us
    all_gather x1, waiting for transfers between devices, per_device(): key_piece = lax.all_gather(key_here, 'seq', axis=0, tiled=True)  243 us
    all_gather x1, waiting for transfers between devices, per_device(): value_piece = lax.all_gather(value_here, 'seq', axis=0, tiled=True)  194 us
    all_to_all x1, waiting for transfers between devices, per_device(): lax.all_to_all(outgoing.reshape(seq_count, capacity, target_width).astype...  40.9 us
  transfers between devices with their start and end apart: 9, of which 6 were waited for; matrix products, arithmetic and copies ran while one was open for 10% of the time, Pallas kernels for 0%

commit v1 on v0

--- a/solution.py
+++ b/solution.py
@@ -132,7 +132,8 @@
         jnp.full((head_count, frame_count), -1e30, jnp.float32),
     )
     running = initial
-    key_piece = lax.all_gather(key_here, "seq", axis=0, tiled=True)
+    sent = jnp.stack([key_here] * lax.axis_size("seq"))
+    key_piece = jnp.concatenate(lax.all_to_all(sent, "seq", 0, 0), axis=0)
     value_piece = lax.all_gather(value_here, "seq", axis=0, tiled=True)
     row_count = key_piece.shape[0]
 

time: 1310 us -> 1170 us (0.89)
  waiting for transfers between devices: 1050 us -> 868 us
  local copies, waits for them, and re-layouts: 97.4 us -> 116 us
  starting transfers between devices: 38.1 us -> 54.4 us
    all_gather x1 -> x0, waiting for transfers between devices: 243 us -> none  [per_device(): key_piece = lax.all_gather(key_here, 'seq', axis=0, tiled=True)]
    all_gather x1, waiting for transfers between devices: 194 us -> 257 us  [per_device(): value_piece = lax.all_gather(value_here, 'seq', axis=0, tiled=True)]
  transfers between devices with their start and end apart: 9 -> 9, of which waited for: 6 -> 4; matrix products, arithmetic and copies ran while one was open for 10% -> 15% of each run, Pallas kernels for 0% -> 0%
where the time goes in v1:
time: 1170 us; the launch traced here: 1160 us
  waiting for transfers between devices  868 us (74%)
  local copies, waits for them, and re-layouts  116 us (10%)
  starting transfers between devices  54.4 us (5%)
  other arithmetic  48.6 us (4%)
  matrix products  32.3 us (3%)
  blocking collectives  28 us (2%)
  between operations  14.6 us (1%)
    psum x1, waiting for transfers between devices, per_device(): proj_grad = lax.psum(proj_term, 'seq')  541 us
    all_gather x1, waiting for transfers between devices, per_device(): value_piece = lax.all_gather(value_here, 'seq', axis=0, tiled=True)  257 us
    all_to_all x1, waiting for transfers between devices, per_device(): lax.all_to_all(outgoing.reshape(seq_count, capacity, target_width).astype...  41.1 us
    reduce_scatter x1, waiting for transfers between devices, per_device(): lax.psum_scatter(jnp.dot(attended, out_weight, preferred_element_type=jnp...  29.2 us
  transfers between devices with their start and end apart: 9, of which 4 were waited for; matrix products, arithmetic and copies ran while one was open for 15% of the time, Pallas kernels for 0%

profile of v1, /device:TPU:8, one launch (start us, length us, event | category | flops | bytes accessed | tf_op | source)
XLA Modules:
  0.0 1162.8 jit_solution(13233743577178564869)
XLA Ops:
  8.2 3.4 collective-permute-start
  11.6 3.3 collective-permute-start.1
  16.7 18.1 %reduce-window.6 = s32[64,13,128]{2,1,0:T(8,128)S(1)} reduce-window(s32[64,13,128]{2,1,0:T(8,128)S(1)} %reshape.253, s32[]{:T(128)} %constant.57.clone.1), window={size=1x1x128 pad=0_0x0_0x127_0}, to_apply=%region_7.8 | reduce-window | flops 13524992 | bytes 851972 | tf_op jit(solution)/shard_map/reduce-window
  36.0 8.8 scatter_custom_fusion
  45.6 12.8 %all-to-all-start.1 = ((s32[64,1,50]{2,1,0:T(1,128)}), s32[64,1,50]{2,1,0:T(1,128)S(1)}, u32[]{:S(2)}, u32[]{:S(2)}) async-start(s32[64,1,50]{2,1,0:T(1,128)} %bitcast.24), calls=%async_computation.2 | async-start | bytes 65536 | tf_op jit(solution)/shard_map/all_to_all | solution.py:193
  58.7 10.7 copy.42
  72.9 17.3 %fusion.67 = f32[1,129,2,120]{3,0,2,1:T(1,128)S(1)} fusion(bf16[1,256,2,120]{3,0,2,1:T(2,128)(2,1)S(1)} %copy.41, bf16[2,120,120,128]{2,1,0,3:T(8,128)(2,1)} %copy.42), kind=kOutput, calls=%fused_computation.134 | convolution fusion | flops 951091200 | bytes 7619520 | tf_op jit(solution)/shard_map/conv_general_dilated | solution.py:108
  90.6 7.8 all_gather.9
  100.4 2.5 stack.3
  102.9 11.5 all-to-all-start
  117.5 9.9 gather_fusion.2
  129.4 257.1 %all-gather.4.cloned.1.call-done = bf16[8192,240]{0,1:T(8,128)(2,1)} async-done(((bf16[128,240]{0,1:T(8,128)(2,1)}), bf16[8192,240]{0,1:T(8,128)(2,1)}) %all-gather.4.cloned.1.call-update) | async-done | bytes 3932176 | tf_op jit(solution)/shard_map/all_gather | solution.py:137
  386.5 4.4 copy.77
  390.9 11.3 all-to-all-start.2
  402.5 5.1 copy.45
  407.6 7.2 reshape_reshape.3
  414.8 6.3 copy.48
  421.1 29.4 %while.15 = (s32[]{:T(128)}, f32[2,128,120]{1,2,0:T(8,128)S(1)}, f32[2,128]{1,0:T(2,128)S(1)}, f32[2,128]{1,0:T(2,128)S(1)}, bf16[16,512,240]{1,2,0:T(8,128)(2,1...) while((s32[]{:T(128)}, f32[2,128,120]{1,2,0:T(8,128)S(1)}, ...), condition=%wide.region_5.6_spmd.clone, body=%wide.region_2.5_spmd.clone.sunk | while | flops 63794432 | bytes 3371117 | solution.py:146
  452.3 2.5 reshape.247
  454.8 5.6 gather_fusion.3
  461.0 29.2 %reduce-scatter.2.cloned.1.call-done = bf16[128,240]{0,1:T(8,128)(2,1)} async-done(((bf16[128,960]{0,1:T(8,128)(2,1)}), bf16[128,240]{0,1:T(8,128)(2,1)}) %reduce-scatter.2.cloned.1.call-update) | async-done | bytes 61456 | tf_op jit(solution)/shard_map/reduce_scatter | solution.py:161
  491.8 6.7 all-gather.1
  499.7 13.5 %all-reduce.1 = (f32[16,101]{1,0:T(8,128)S(1)}, f32[16]{0:T(128)S(1)}, f32[16,101]{1,0:T(8,128)S(1)}) all-reduce(f32[16,101]{1,0:T(8,128)S(1)} %fusion.7, f32[16]{0:T(128)S(1)} %get-tuple-element.115, f32[16,101]{1,0:T(8,128)S(1)} %bitcast.169), channel_id=1, replica_groups=mesh['seq'=64,'head'=4] {'head'}, use_global_device_ids=true, to_apply=%region_15.16 | all-reduce | flops 3248 | bytes 25984 | tf_op jit(solution)/shard_map/psum | solution.py:203
  517.1 13.0 %scatter_custom_fusion.1 = f32[3200,256]{1,0:T(8,128)} fusion(s32[1600]{0:T(1024)S(1)} %fusion.54, f32[1600,256]{1,0:T(8,128)} %reshape.300, f32[]{:T(128)} %constant.68.clone.1), kind=kCustom, calls=%fused_computation.28 | custom fusion | bytes 3277312 | tf_op jit(solution)/shard_map/scatter | solution.py:218
  530.0 2.1 convert_element_type.73
  533.6 11.5 all-to-all-start.3
  545.7 1.6 fusion.43
  548.4 41.1 %all-to-all-done.3 = bf16[64,50,256]{2,1,0:T(8,128)(2,1)S(1)} async-done(((bf16[64,50,256]{2,1,0:T(8,128)(2,1)}), bf16[64,50,256]{2,1,0:T(8,128)(2,1)S(1)}, u32[]{:S(2)}, u32[]{:S(2)}) %all-to-all-start.3) | async-done | bytes 1638432 | tf_op jit(solution)/shard_map/all_to_all | solution.py:221
  589.5 1.9 reshape.308
  591.4 20.7 %scatter_custom_fusion.2 = f32[129,256]{1,0:T(8,128)S(1)} fusion(s32[3200]{0:T(1024)S(1)} %fusion.48, f32[3200,256]{1,0:T(8,128)} %reshape.308, f32[]{:T(128)} %constant.68.clone.1), kind=kCustom, calls=%fused_computation.77 | custom fusion | flops 819200 | bytes 132608 | tf_op jit(solution)/shard_map/scatter-add | solution.py:86
  612.9 540.9 %all-reduce.4.cloned.1.call-done = f32[960,256]{1,0:T(8,128)} async-done(((f32[960,256]{1,0:T(8,128)}), f32[960,256]{1,0:T(8,128)}) %all-reduce.4.cloned.1.call-update) | async-done | bytes 983056 | tf_op jit(solution)/shard_map/psum | solution.py:235
  1153.8 2.2 copy.93
  (226 shorter events, 57.4 us)
Async XLA Ops:
  7.2 443.4 %copy-start = (bf16[240,960]{1,0:T(8,128)(2,1)S(1)}, bf16[240,960]{1,0:T(8,128)(2,1)}, u32[]{:S(2)}) copy-start(bf16[240,960]{1,0:T(8,128)(2,1)} %param.22) | copy-start | bytes 1382404
  8.2 64.3 %collective-permute-start = (bf16[64,240]{0,1:T(8,128)(2,1)S(1)}, bf16[64,240]{0,1:T(8,128)(2,1)S(1)}, u32[]{:S(2)}, u32[]{:S(2)}) collective-permute-start(bf16[64,240]{0,1:T(8,128)(2,1)S(1)} %get-tuple-element.106), channel_id=1, source_target_pairs={{0,4},{4,8},{8,12},{12,16},{16,20},{20,24},{24,28},{28,32},{32,36}... | collective-permute-start | bytes 92168 | tf_op jit(solution)/shard_map/ppermute | solution.py:20
  11.6 60.9 %collective-permute-start.1 = (bf16[64,240]{0,1:T(8,128)(2,1)S(1)}, bf16[64,240]{0,1:T(8,128)(2,1)S(1)}, u32[]{:S(2)}, u32[]{:S(2)}) collective-permute-start(bf16[64,240]{0,1:T(8,128)(2,1)S(1)} %get-tuple-element.107), channel_id=1, source_target_pairs={{4,0},{8,4},{12,8},{16,12},{20,16},{24,20},{28,24},{32,28},{36,32}... | collective-permute-start | bytes 92168 | tf_op jit(solution)/shard_map/ppermute | solution.py:21
  45.6 54.8 %all-to-all-start.1 = ((s32[64,1,50]{2,1,0:T(1,128)}), s32[64,1,50]{2,1,0:T(1,128)S(1)}, u32[]{:S(2)}, u32[]{:S(2)}) async-start(s32[64,1,50]{2,1,0:T(1,128)} %bitcast.24), calls=%async_computation.2 | async-start | bytes 65536 | tf_op jit(solution)/shard_map/all_to_all | solution.py:193
  58.4 328.2 %all-gather.4.cloned.1.call-start = ((), (), s32[]{:S(2)}) async-start(), calls=%async_computation.5 | async-start | bytes 3993600 | tf_op jit(solution)/shard_map/all_gather | solution.py:137
  58.7 10.8 copy-start.5
  69.5 1.5 copy-start.6
  69.5 3.1 copy-start.3
  72.8 25.8 %copy-start.11 = (f32[960]{0:T(1024)S(1)}, f32[960]{0:T(1024)}, u32[]{:S(2)}) copy-start(f32[960]{0:T(1024)} %param.18) | copy-start | bytes 11524
  72.8 25.8 %copy-start.12 = (f32[960]{0:T(1024)S(1)}, f32[960]{0:T(1024)}, u32[]{:S(2)}) copy-start(f32[960]{0:T(1024)} %param.17) | copy-start | bytes 11524
  102.9 11.6 copy-start.7
  102.9 288.1 %all-to-all-start = ((bf16[64,128,240]{1,2,0:T(8,128)(2,1)}), bf16[64,128,240]{1,2,0:T(8,128)(2,1)}, u32[]{:S(2)}, u32[]{:S(2)}) async-start(bf16[64,128,240]{1,2,0:T(8,128)(2,1)} %stack.3), calls=%async_computation | async-start | bytes 7864320 | tf_op jit(solution)/shard_map/all_to_all | solution.py:136
  114.4 3.1 copy-start.1
  390.9 61.4 %all-to-all-start.2 = ((bf16[64,50,256]{2,1,0:T(8,128)(2,1)}), bf16[64,50,256]{2,1,0:T(8,128)(2,1)}, u32[]{:S(2)}, u32[]{:S(2)}) async-start(bf16[64,50,256]{2,1,0:T(8,128)(2,1)} %reshape.273), calls=%async_computation.3 | async-start | bytes 3670016 | tf_op jit(solution)/shard_map/all_to_all | solution.py:195
  402.3 88.0 %reduce-scatter.2.cloned.1.call-start = ((), (), s32[]{:S(2)}) async-start(), calls=%async_computation.6 | async-start | bytes 307200 | tf_op jit(solution)/shard_map/reduce_scatter | solution.py:161
  421.1 30.6 %copy-start.13 = (s32[16]{0:T(128)S(1)}, s32[16]{0:T(128)}, u32[]{:S(2)}) copy-start(s32[16]{0:T(128)} %param.25) | copy-start | bytes 196
  460.4 38.2 %copy-start.4 = (bf16[960,256]{1,0:T(8,128)(2,1)S(1)}, bf16[960,256]{1,0:T(8,128)(2,1)}, u32[]{:S(2)}) copy-start(bf16[960,256]{1,0:T(8,128)(2,1)} %param.23) | copy-start | bytes 1474564
  460.6 52.8 %copy-start.10 = (f32[16]{0:T(128)S(1)}, f32[16]{0:T(128)}, u32[]{:S(2)}) copy-start(f32[16]{0:T(128)} %param.27) | copy-start | bytes 196
  491.1 23.3 %copy-start.8 = (bf16[128,240]{0,1:T(8,128)(2,1)}, bf16[128,240]{0,1:T(8,128)(2,1)S(1)}, u32[]{:S(2)}) copy-start(bf16[128,240]{0,1:T(8,128)(2,1)S(1)} %add_convert_fusion) | copy-start | bytes 184324
  514.4 1.2 copy-start.2
  533.6 55.9 %all-to-all-start.3 = ((bf16[64,50,256]{2,1,0:T(8,128)(2,1)}), bf16[64,50,256]{2,1,0:T(8,128)(2,1)S(1)}, u32[]{:S(2)}, u32[]{:S(2)}) async-start(bf16[64,50,256]{2,1,0:T(8,128)(2,1)} %convert_element_type.74), calls=%async_computation.4 | async-start | bytes 3670016 | tf_op jit(solution)/shard_map/all_to_all | solution.py:221
  545.1 608.8 %all-reduce.4.cloned.1.call-start = ((), (), s32[]{:S(2)}) async-start(), calls=%async_computation.7 | async-start | bytes 1966080 | tf_op jit(solution)/shard_map/psum | solution.py:235
  612.9 543.1 %copy-start.9 = (f32[128,256]{1,0:T(8,128)}, f32[128,256]{1,0:T(8,128)S(1)}, u32[]{:S(2)}) copy-start(f32[128,256]{1,0:T(8,128)S(1)} %scatter_custom_fusion.3) | copy-start | bytes 393220
Sparse Core Ops, SparseCore 0:
  100.0 286.5 all-gather.3
  451.8 38.4 reduce-scatter.1
  549.3 604.4 all-reduce.3
